TPU v7x, 256 devices: a whole 4x4x8 slice. The times are simulated.
256 devices in a mesh: lon: 32 (over x_hi, z, core), lat: 8 (over x_lo, y).
Axes of the slice: x: 4 (x_hi: 2, x_lo: 2; x = x_hi * 2 + x_lo), y: 4, z: 8, core: 2. Of those that a mesh axis runs over, the one named last changes fastest.
Arguments:
- tracer_start: float32 [3, 16, 128, 4096], P(None, None, 'lat', 'lon'), may hold values from -6 to 6
- source: float32 [3, 16, 128, 4096], P(None, None, 'lat', 'lon'), may hold values from -3 to 3
- target: float32 [3, 16, 128, 4096], P(None, None, 'lat', 'lon'), may hold values from -27 to 27
- east_vel: float32 [16, 128, 4096], P(None, 'lat', 'lon'), may hold values from -0.12 to 0.12
- north_vel: float32 [16, 128, 4096], P(None, 'lat', 'lon'), may hold values from -0.12 to 0.12
- vertical_vel: float32 [16, 128, 4096], P(None, 'lat', 'lon'), may hold values from -0.12 to 0.12
- diffusivity: float32 [16, 128, 4096], P(None, 'lat', 'lon'), may hold values from 0.01 to 0.04
- sea_mask: int32 [16, 128, 4096], P(None, 'lat', 'lon'), may hold values 0 or 1
- reaction_rate: float32 [3, 16], replicated, may hold values from 0.05 to 0.5
- fold_partner: int32 [4096], P('lon'), may hold values from 0 to 4095, as said below
Outputs:
- source_grad: float32 [3, 16, 128, 4096], P(None, None, 'lat', 'lon')
- grad_norm: float32 [], replicated
Inputs may be any that keep to these rules, and one draw needn't show every extreme that they name: fold_partner[fold_partner[i]] = i; column i meets column (s - i) mod 4096 across the fold, for one s of each draw.
All inputs are finite; a program needn't handle non-finite values. No bound on the sum of `sea_mask` on one device may be relied on, other than what follows from the above.
Results may differ from a plain program's by a relative error of at most 0.00002.
Values sent between devices are 32-bit elements; how exact they have to be, the bound alone decides.
No kernel may reach another device: no remote copies, remote signals or barrier semaphores. Data moves between devices by JAX's collectives and lax.ppermute only.
A program may use at most 64 MiB of HBM per device.

v0:
```python
import jax
import jax.numpy as jnp
from jax import lax
from jax.sharding import PartitionSpec as P

STEPS = 4


def with_halo(block, sides, width, periodic):
    for axis, dim in sides:
        count = lax.axis_size(axis)
        forward = [(i, i + 1) for i in range(count - 1)]
        if periodic:
            forward.append((count - 1, 0))
        backward = [(target, source) for source, target in forward]
        low = lax.ppermute(
            lax.slice_in_dim(block, block.shape[dim] - width, None, axis=dim), axis, forward
        )
        high = lax.ppermute(lax.slice_in_dim(block, 0, width, axis=dim), axis, backward)
        block = jnp.concatenate([low, block, high], axis=dim)
    return block


def upwind_pair(velocity, mixing, face_sea):
    flow_rate = velocity * face_sea
    mixing_part = mixing * face_sea
    return (jnp.maximum(flow_rate, 0.0) + mixing_part, jnp.minimum(flow_rate, 0.0) - mixing_part)


def on_device(
    tracer_start,
    source,
    target,
    east_vel,
    north_vel,
    vertical_vel,
    diffusivity,
    sea_mask,
    reaction_rate,
    fold_partner,
):
    ocean = sea_mask.astype(jnp.float32)
    statics = jnp.stack([east_vel, north_vel, diffusivity, ocean])
    wide_static = with_halo(statics, (("lon", 3),), 1, True)
    tall_static = with_halo(statics, (("lat", 2),), 1, False)
    west_cell = wide_static[..., :-1]
    east_cell = wide_static[..., 1:]
    east_own, east_next = upwind_pair(
        west_cell[0], 0.5 * (west_cell[2] + east_cell[2]), west_cell[3] * east_cell[3]
    )
    below_row = tall_static[:, :, :-1, :]
    above_row = tall_static[:, :, 1:, :]
    north_own, north_next = upwind_pair(
        below_row[1], 0.5 * (below_row[2] + above_row[2]), below_row[3] * above_row[3]
    )
    up_own, up_next = upwind_pair(
        vertical_vel[:-1], 0.5 * (diffusivity[:-1] + diffusivity[1:]), ocean[:-1] * ocean[1:]
    )
    top_static = jnp.stack([north_vel[:, -1, :], diffusivity[:, -1, :], ocean[:, -1, :]])
    fold_all = lax.all_gather(top_static, "lon", axis=2, tiled=True)
    across = jnp.take(fold_all, fold_partner, axis=2)
    north_top = (lax.axis_index("lat") == lax.axis_size("lat") - 1).astype(jnp.float32)
    fold_own, fold_next = upwind_pair(
        0.5 * (top_static[0] - across[0]),
        0.5 * (top_static[1] + across[1]),
        top_static[2] * across[2] * north_top,
    )
    decay_rate = reaction_rate[:, :, None, None]

    def neighbours(quantity):
        east_west = with_halo(quantity, (("lon", 3),), 1, True)
        south_north = with_halo(quantity, (("lat", 2),), 1, False)
        top_row = quantity[:, :, -1, :]
        whole_top = lax.all_gather(top_row, "lon", axis=2, tiled=True)
        partner_row = jnp.take(whole_top, fold_partner, axis=2)
        return (east_west, south_north, partner_row)

    kept_states = [tracer_start]
    for repeat in range(STEPS):
        advance_quantity = kept_states[-1]
        uptake = decay_rate * advance_quantity / jnp.sqrt(1.0 + advance_quantity * advance_quantity)
        divergence_east_west, divergence_south_north, divergence_partner_row = neighbours(
            advance_quantity
        )
        east_flux = (
            east_own * divergence_east_west[..., :-1] + east_next * divergence_east_west[..., 1:]
        )
        north_flux = (
            north_own * divergence_south_north[:, :, :-1, :]
            + north_next * divergence_south_north[:, :, 1:, :]
        )
        divergence_top_row = advance_quantity[:, :, -1, :]
        fold_flux = fold_own * divergence_top_row + fold_next * divergence_partner_row
        north_flux = north_flux.at[:, :, -1, :].add(fold_flux)
        up_flux = up_own * advance_quantity[:, :-1] + up_next * advance_quantity[:, 1:]
        zero_level = jnp.zeros_like(advance_quantity[:, :1])
        vertical_part = jnp.concatenate([up_flux, zero_level], 1) - jnp.concatenate(
            [zero_level, up_flux], 1
        )
        kept_states.append(
            ocean
            * (
                advance_quantity
                - (
                    east_flux[..., 1:]
                    - east_flux[..., :-1]
                    + (north_flux[:, :, 1:, :] - north_flux[:, :, :-1, :])
                    + vertical_part
                )
                - uptake
                + source
            )
        )
    last_state = kept_states[-1]
    adjoint = ocean * (last_state - target)
    source_grad = ocean * adjoint
    for backward in range(STEPS - 1, 0, -1):
        current = kept_states[backward]
        weight = ocean * adjoint
        transposed_east_west, transposed_south_north, transposed_partner_row = neighbours(weight)
        east_diff = transposed_east_west[..., :-1] - transposed_east_west[..., 1:]
        north_diff = transposed_south_north[:, :, :-1, :] - transposed_south_north[:, :, 1:, :]
        up_diff = weight[:, :-1] - weight[:, 1:]
        result = east_own[..., 1:] * east_diff[..., 1:] + east_next[..., :-1] * east_diff[..., :-1]
        result = result + (
            north_own[:, 1:, :] * north_diff[:, :, 1:, :]
            + north_next[:, :-1, :] * north_diff[:, :, :-1, :]
        )
        result = result.at[:, :, -1, :].add(
            fold_own * (weight[:, :, -1, :] - transposed_partner_row)
        )
        transposed_zero_level = jnp.zeros_like(weight[:, :1])
        result = result + (
            jnp.concatenate([up_own * up_diff, transposed_zero_level], 1)
            + jnp.concatenate([transposed_zero_level, up_next * up_diff], 1)
        )
        spread = 1.0 + current * current
        adjoint = weight - result - decay_rate / (spread * jnp.sqrt(spread)) * weight
        source_grad = source_grad + ocean * adjoint
    squares = lax.psum(jnp.sum(source_grad * source_grad), ("lon", "lat"))
    return (source_grad, jnp.sqrt(squares))


def solution(mesh):
    return jax.shard_map(
        on_device,
        mesh=mesh,
        in_specs=(
            P(None, None, "lat", "lon"),
            P(None, None, "lat", "lon"),
            P(None, None, "lat", "lon"),
            P(None, "lat", "lon"),
            P(None, "lat", "lon"),
            P(None, "lat", "lon"),
            P(None, "lat", "lon"),
            P(None, "lat", "lon"),
            P(),
            P("lon"),
        ),
        out_specs=(P(None, None, "lat", "lon"), P()),
        check_vma=False,
    )
```

profile of v0, /device:TPU:1, one launch (start us, length us, event | category | flops | bytes accessed | tf_op | source)
XLA Modules:
  0.0 698.3 jit_solution(13284979570440464098)
XLA Ops:
  0.6 1.9 fusion.105
  3.1 4.6 collective-permute-start.6
  15.2 1.5 collective-permute-start
  19.7 2.2 fusion.104
  23.0 48.5 %all-gather = f32[3,16,1,4096]{3,1,2,0:T(8,128)} all-gather(f32[3,16,1,128]{3,1,2,0:T(8,128)S(1)} %get-tuple-element.158), channel_id=2, replica_groups=mesh['lon'=32,'lat'=8] {'lon'}, dimensions={3}, use_global_device_ids=true | all-gather | bytes 811008 | tf_op jit(solution)/shard_map/all_gather | solution.py:74
  71.5 39.1 %all_gather.24 = f32[3,16,4096]{2,1,0:T(8,128)S(1)} all-gather(f32[3,16,128]{2,1,0:T(8,128)S(1)} %pad_maximum_fusion.12), channel_id=1, replica_groups=mesh['lon'=32,'lat'=8] {'lon'}, dimensions={2}, use_global_device_ids=true | all-gather | bytes 811008 | tf_op jit(solution)/shard_map/all_gather | solution.py:60
  110.6 5.8 copy.549
  116.5 4.2 gather_fusion
  122.8 6.9 copy.552
  129.7 4.1 gather_fusion.1
  135.8 1.4 add_bitcast_fusion
  137.3 3.5 collective-permute-done.2
  140.8 4.7 collective-permute-start.4
  149.0 2.5 multiply_add_fusion.2
  152.6 3.6 collective-permute-start.10
  157.6 3.8 collective-permute-start.8
  161.3 2.6 collective-permute-start.9
  164.8 49.4 %all-gather.1 = f32[3,16,1,4096]{3,1,2,0:T(8,128)} all-gather(f32[3,16,1,128]{3,1,2,0:T(8,128)S(1)} %get-tuple-element.153), channel_id=3, replica_groups=mesh['lon'=32,'lat'=8] {'lon'}, dimensions={3}, use_global_device_ids=true | all-gather | bytes 811008 | tf_op jit(solution)/shard_map/all_gather | solution.py:74
  214.2 6.8 copy.567
  221.1 4.3 gather_fusion.2
  227.8 2.9 fusion.11
  230.7 1.8 fusion.31
  233.6 4.3 collective-permute-start.14
  239.8 50.3 %all-gather.2 = f32[3,16,1,4096]{3,1,2,0:T(8,128)} all-gather(f32[3,16,1,128]{3,1,2,0:T(8,128)S(1)} %get-tuple-element.148), channel_id=4, replica_groups=mesh['lon'=32,'lat'=8] {'lon'}, dimensions={3}, use_global_device_ids=true | all-gather | bytes 811008 | tf_op jit(solution)/shard_map/all_gather | solution.py:74
  290.1 6.8 copy.585
  296.9 4.9 gather_fusion.3
  305.7 2.6 fusion.17
  311.2 4.3 collective-permute-start.18
  317.4 50.3 %all-gather.3 = f32[3,16,1,4096]{3,1,2,0:T(8,128)} all-gather(f32[3,16,1,128]{3,1,2,0:T(8,128)S(1)} %get-tuple-element.143), channel_id=5, replica_groups=mesh['lon'=32,'lat'=8] {'lon'}, dimensions={3}, use_global_device_ids=true | all-gather | bytes 811008 | tf_op jit(solution)/shard_map/all_gather | solution.py:74
  367.7 6.8 copy.597
  374.5 4.9 gather_fusion.4
  384.4 1.6 fusion.16
  388.3 6.1 collective-permute-start.22
  396.5 50.1 %all-gather.4 = f32[3,16,1,4096]{3,1,2,0:T(8,128)} all-gather(f32[3,16,1,128]{3,1,2,0:T(8,128)S(1)} %get-tuple-element.137), channel_id=6, replica_groups=mesh['lon'=32,'lat'=8] {'lon'}, dimensions={3}, use_global_device_ids=true | all-gather | bytes 811008 | tf_op jit(solution)/shard_map/all_gather | solution.py:74
  446.6 6.9 copy.618
  453.5 4.9 gather_fusion.5
  465.2 6.4 collective-permute-start.26
  473.5 50.1 %all-gather.5 = f32[3,16,1,4096]{3,1,2,0:T(8,128)} all-gather(f32[3,16,1,128]{3,1,2,0:T(8,128)S(1)} %get-tuple-element.130), channel_id=7, replica_groups=mesh['lon'=32,'lat'=8] {'lon'}, dimensions={3}, use_global_device_ids=true | all-gather | bytes 811008 | tf_op jit(solution)/shard_map/all_gather | solution.py:74
  523.5 6.8 copy.631
  530.4 4.9 gather_fusion.6
  538.1 1.5 fusion.55
  541.6 6.4 collective-permute-start.30
  549.9 47.6 %all-gather.6 = f32[3,16,1,4096]{3,1,2,0:T(8,128)S(1)} all-gather(f32[3,16,1,128]{3,1,2,0:T(8,128)S(1)} %get-tuple-element.120), channel_id=8, replica_groups=mesh['lon'=32,'lat'=8] {'lon'}, dimensions={3}, use_global_device_ids=true | all-gather | bytes 811008 | tf_op jit(solution)/shard_map/all_gather | solution.py:74
  597.6 5.8 copy.645
  603.4 4.3 gather_fusion.7
  607.8 1.4 maximum_subtract_fusion.2
  609.5 3.0 multiply_reduce_fusion
  612.6 83.9 %psum.7 = f32[]{:T(128)} all-reduce(f32[]{:T(128)} %get-tuple-element.93), channel_id=1, replica_groups=mesh['lon'=32,'lat'=8] {'lon','lat'}, use_global_device_ids=true, to_apply=%region_1.3 | all-reduce | flops 1 | bytes 8 | tf_op jit(solution)/shard_map/psum | solution.py:140
  (187 shorter events, 61.7 us)
Async XLA Ops:
  3.1 144.9 %collective-permute-start.6 = (f32[3,16,1,128]{3,1,0,2:T(8,128)}, f32[3,16,1,128]{3,1,0,2:T(8,128)}, u32[]{:S(2)}, u32[]{:S(2)}) collective-permute-start(f32[3,16,1,128]{3,1,0,2:T(8,128)} %get-tuple-element.160), channel_id=1, source_target_pairs={{0,1},{1,2},{2,3},{3,4},{4,5},{5,6},{6,7},{8,9},{9,10},{10,11},{11... | collective-permute-start | bytes 73736 | tf_op jit(solution)/shard_map/ppermute | solution.py:16
  7.8 140.3 %collective-permute-start.7 = (f32[3,16,1,128]{3,1,0,2:T(8,128)}, f32[3,16,1,128]{3,1,0,2:T(8,128)}, u32[]{:S(2)}, u32[]{:S(2)}) collective-permute-start(f32[3,16,1,128]{3,1,0,2:T(8,128)} %get-tuple-element.159), channel_id=1, source_target_pairs={{1,0},{2,1},{3,2},{4,3},{5,4},{6,5},{7,6},{9,8},{10,9},{11,10},{12... | collective-permute-start | bytes 73736 | tf_op jit(solution)/shard_map/ppermute | solution.py:19
  10.0 110.8 %copy-start = (f32[3,16,16,128]{3,2,1,0:T(8,128)S(1)}, f32[3,16,16,128]{3,2,1,0:T(8,128)}, u32[]{:S(2)}) copy-start(f32[3,16,16,128]{3,2,1,0:T(8,128)} %param.26) | copy-start | bytes 1179652
  11.8 134.2 %collective-permute-start.5 = (f32[4,16,1,128]{3,2,1,0:T(1,128)}, f32[4,16,1,128]{3,2,1,0:T(1,128)}, u32[]{:S(2)}, u32[]{:S(2)}) collective-permute-start(f32[4,16,1,128]{3,2,1,0:T(1,128)} %get-tuple-element.119), channel_id=1, source_target_pairs={{1,0},{2,1},{3,2},{4,3},{5,4},{6,5},{7,6},{9,8},{10,9},{11,10},{12... | collective-permute-start | bytes 98312 | tf_op jit(solution)/shard_map/ppermute | solution.py:19
  14.2 120.3 %collective-permute-start.1 = (f32[4,16,16,1]{3,2,1,0:T(8,128)}, f32[4,16,16,1]{3,2,1,0:T(8,128)}, u32[]{:S(2)}, u32[]{:S(2)}) collective-permute-start(f32[4,16,16,1]{3,2,1,0:T(8,128)} %get-tuple-element.117), channel_id=1, source_target_pairs={{8,0},{16,8},{24,16},{32,24},{40,32},{48,40},{56,48},{64,56},{72,6... | collective-permute-start | bytes 12296 | tf_op jit(solution)/shard_map/ppermute | solution.py:19
  15.2 120.6 %collective-permute-start = (f32[4,16,16,1]{3,2,1,0:T(8,128)}, f32[4,16,16,1]{3,2,1,0:T(8,128)}, u32[]{:S(2)}, u32[]{:S(2)}) collective-permute-start(f32[4,16,16,1]{3,2,1,0:T(8,128)} %get-tuple-element.116), channel_id=1, source_target_pairs={{0,8},{8,16},{16,24},{24,32},{32,40},{40,48},{48,56},{56,64},{64,7... | collective-permute-start | bytes 12296 | tf_op jit(solution)/shard_map/ppermute | solution.py:16
  19.7 103.0 %copy-start.12 = (pred[128]{0:T(512)(128)(4,1)}, pred[128]{0:T(512)(128)(4,1)S(1)}, u32[]{:S(2)}) copy-start(pred[128]{0:T(512)(128)(4,1)S(1)} %compare_and_fusion) | copy-start | bytes 388
  71.5 58.1 %copy-start.16 = (s32[1024]{0:T(1024)}, s32[1024]{0:T(1024)S(1)}, u32[]{:S(2)}) copy-start(s32[1024]{0:T(1024)S(1)} %pad_clamp_fusion) | copy-start | bytes 12292
  116.5 19.3 %copy-start.4 = (f32[16,16,128]{2,1,0:T(8,128)S(1)}, f32[16,16,128]{2,1,0:T(8,128)}, u32[]{:S(2)}) copy-start(f32[16,16,128]{2,1,0:T(8,128)} %param.32) | copy-start | bytes 393220
  116.5 19.3 %copy-start.6 = (f32[16,16,128]{2,1,0:T(8,128)S(1)}, f32[16,16,128]{2,1,0:T(8,128)}, u32[]{:S(2)}) copy-start(f32[16,16,128]{2,1,0:T(8,128)} %param.30) | copy-start | bytes 393220
  116.5 19.3 %copy-start.7 = (f32[16,16,128]{2,1,0:T(8,128)S(1)}, f32[16,16,128]{2,1,0:T(8,128)}, u32[]{:S(2)}) copy-start(f32[16,16,128]{2,1,0:T(8,128)} %param.29) | copy-start | bytes 393220
  122.6 41.3 %copy-start.2 = (f32[15,16,128]{2,0,1:T(8,128)}, f32[15,16,128]{2,0,1:T(8,128)S(1)}, u32[]{:S(2)}) copy-start(f32[15,16,128]{2,0,1:T(8,128)S(1)} %copy.662) | copy-start | bytes 368644
  122.7 41.3 %copy-start.3 = (f32[15,16,128]{2,0,1:T(8,128)}, f32[15,16,128]{2,0,1:T(8,128)S(1)}, u32[]{:S(2)}) copy-start(f32[15,16,128]{2,0,1:T(8,128)S(1)} %copy.661) | copy-start | bytes 368644
  122.8 26.2 %copy-start.1 = (f32[3,16,16,128]{3,2,1,0:T(8,128)S(1)}, f32[3,16,16,128]{3,2,1,0:T(8,128)}, u32[]{:S(2)}) copy-start(f32[3,16,16,128]{3,2,1,0:T(8,128)} %param.27) | copy-start | bytes 1179652
  134.5 14.4 %copy-start.13 = (pred[128]{0:T(512)(128)(4,1)S(1)}, pred[128]{0:T(512)(128)(4,1)}, u32[]{:S(2)}) copy-start(pred[128]{0:T(512)(128)(4,1)} %copy-done.12) | copy-start | bytes 388
  134.5 6.3 collective-permute-start.2
  135.8 9.7 %collective-permute-start.3 = (f32[3,16,16,1]{3,2,1,0:T(8,128)}, f32[3,16,16,1]{3,2,1,0:T(8,128)S(1)}, u32[]{:S(2)}, u32[]{:S(2)}) collective-permute-start(f32[3,16,16,1]{3,2,1,0:T(8,128)} %get-tuple-element.156), channel_id=1, source_target_pairs={{8,0},{16,8},{24,16},{32,24},{40,32},{48,40},{56,48},{64,56},{72,6... | collective-permute-start | bytes 9224 | tf_op jit(solution)/shard_map/ppermute | solution.py:19
  140.8 6.0 collective-permute-start.4
  152.6 75.1 %collective-permute-start.10 = (f32[3,16,1,128]{3,1,0,2:T(8,128)S(1)}, f32[3,16,1,128]{3,1,0,2:T(8,128)S(1)}, u32[]{:S(2)}, u32[]{:S(2)}) collective-permute-start(f32[3,16,1,128]{3,1,0,2:T(8,128)S(1)} %get-tuple-element.155), channel_id=1, source_target_pairs={{0,1},{1,2},{2,3},{3,4},{4,5},{5,6},{6,7},{8,9},{9,10},{10,11},{11... | collective-permute-start | bytes 73736 | tf_op jit(solution)/shard_map/ppermute | solution.py:16
  156.3 71.5 %collective-permute-start.11 = (f32[3,16,1,128]{3,1,0,2:T(8,128)S(1)}, f32[3,16,1,128]{3,1,0,2:T(8,128)S(1)}, u32[]{:S(2)}, u32[]{:S(2)}) collective-permute-start(f32[3,16,1,128]{3,1,0,2:T(8,128)S(1)} %get-tuple-element.154), channel_id=1, source_target_pairs={{1,0},{2,1},{3,2},{4,3},{5,4},{6,5},{7,6},{9,8},{10,9},{11,10},{12... | collective-permute-start | bytes 73736 | tf_op jit(solution)/shard_map/ppermute | solution.py:19
  157.6 68.6 %collective-permute-start.8 = (f32[3,16,16,1]{3,2,1,0:T(8,128)}, f32[3,16,16,1]{3,2,1,0:T(8,128)}, u32[]{:S(2)}, u32[]{:S(2)}) collective-permute-start(f32[3,16,16,1]{3,2,1,0:T(8,128)} %get-tuple-element.152), channel_id=1, source_target_pairs={{0,8},{8,16},{16,24},{24,32},{32,40},{40,48},{48,56},{56,64},{64,7... | collective-permute-start | bytes 9224 | tf_op jit(solution)/shard_map/ppermute | solution.py:16
  161.3 66.4 %copy-start.14 = (pred[128]{0:T(512)(128)(4,1)S(1)}, pred[128]{0:T(512)(128)(4,1)}, u32[]{:S(2)}) copy-start(pred[128]{0:T(512)(128)(4,1)} %copy-done.12) | copy-start | bytes 388
  161.3 66.5 %copy-start.10 = (f32[3,16]{1,0:T(4,128)S(1)}, f32[3,16]{1,0:T(4,128)}, u32[]{:S(2)}) copy-start(f32[3,16]{1,0:T(4,128)} %param.34) | copy-start | bytes 580
  161.3 64.8 %collective-permute-start.9 = (f32[3,16,16,1]{3,2,1,0:T(8,128)}, f32[3,16,16,1]{3,2,1,0:T(8,128)}, u32[]{:S(2)}, u32[]{:S(2)}) collective-permute-start(f32[3,16,16,1]{3,2,1,0:T(8,128)} %get-tuple-element.151), channel_id=1, source_target_pairs={{8,0},{16,8},{24,16},{32,24},{40,32},{48,40},{56,48},{64,56},{72,6... | collective-permute-start | bytes 9224 | tf_op jit(solution)/shard_map/ppermute | solution.py:19
  233.6 72.0 %collective-permute-start.14 = (f32[3,16,1,128]{3,1,0,2:T(8,128)S(1)}, f32[3,16,1,128]{3,1,0,2:T(8,128)S(1)}, u32[]{:S(2)}, u32[]{:S(2)}) collective-permute-start(f32[3,16,1,128]{3,1,0,2:T(8,128)S(1)} %get-tuple-element.150), channel_id=1, source_target_pairs={{0,1},{1,2},{2,3},{3,4},{4,5},{5,6},{6,7},{8,9},{9,10},{10,11},{11... | collective-permute-start | bytes 73736 | tf_op jit(solution)/shard_map/ppermute | solution.py:16
  237.9 67.8 %collective-permute-start.15 = (f32[3,16,1,128]{3,1,0,2:T(8,128)S(1)}, f32[3,16,1,128]{3,1,0,2:T(8,128)S(1)}, u32[]{:S(2)}, u32[]{:S(2)}) collective-permute-start(f32[3,16,1,128]{3,1,0,2:T(8,128)S(1)} %get-tuple-element.149), channel_id=1, source_target_pairs={{1,0},{2,1},{3,2},{4,3},{5,4},{6,5},{7,6},{9,8},{10,9},{11,10},{12... | collective-permute-start | bytes 73736 | tf_op jit(solution)/shard_map/ppermute | solution.py:19
  239.2 63.7 %collective-permute-start.12 = (f32[3,16,16,1]{3,1,0,2:T(8,128)}, f32[3,16,16,1]{3,1,0,2:T(8,128)}, u32[]{:S(2)}, u32[]{:S(2)}) collective-permute-start(f32[3,16,16,1]{3,1,0,2:T(8,128)} %get-tuple-element.147), channel_id=1, source_target_pairs={{0,8},{8,16},{16,24},{24,32},{32,40},{40,48},{48,56},{56,64},{64,7... | collective-permute-start | bytes 9224 | tf_op jit(solution)/shard_map/ppermute | solution.py:16
  239.3 64.8 %collective-permute-start.13 = (f32[3,16,16,1]{3,1,0,2:T(8,128)}, f32[3,16,16,1]{3,1,0,2:T(8,128)}, u32[]{:S(2)}, u32[]{:S(2)}) collective-permute-start(f32[3,16,16,1]{3,1,0,2:T(8,128)} %get-tuple-element.146), channel_id=1, source_target_pairs={{8,0},{16,8},{24,16},{32,24},{40,32},{48,40},{56,48},{64,56},{72,6... | collective-permute-start | bytes 9224 | tf_op jit(solution)/shard_map/ppermute | solution.py:19
  311.2 73.1 %collective-permute-start.18 = (f32[3,16,1,128]{3,1,0,2:T(8,128)S(1)}, f32[3,16,1,128]{3,1,0,2:T(8,128)S(1)}, u32[]{:S(2)}, u32[]{:S(2)}) collective-permute-start(f32[3,16,1,128]{3,1,0,2:T(8,128)S(1)} %get-tuple-element.145), channel_id=1, source_target_pairs={{0,1},{1,2},{2,3},{3,4},{4,5},{5,6},{6,7},{8,9},{9,10},{10,11},{11... | collective-permute-start | bytes 73736 | tf_op jit(solution)/shard_map/ppermute | solution.py:16
  315.5 68.9 %collective-permute-start.19 = (f32[3,16,1,128]{3,1,0,2:T(8,128)S(1)}, f32[3,16,1,128]{3,1,0,2:T(8,128)S(1)}, u32[]{:S(2)}, u32[]{:S(2)}) collective-permute-start(f32[3,16,1,128]{3,1,0,2:T(8,128)S(1)} %get-tuple-element.144), channel_id=1, source_target_pairs={{1,0},{2,1},{3,2},{4,3},{5,4},{6,5},{7,6},{9,8},{10,9},{11,10},{12... | collective-permute-start | bytes 73736 | tf_op jit(solution)/shard_map/ppermute | solution.py:19
  316.8 63.7 %collective-permute-start.16 = (f32[3,16,16,1]{3,1,0,2:T(8,128)}, f32[3,16,16,1]{3,1,0,2:T(8,128)}, u32[]{:S(2)}, u32[]{:S(2)}) collective-permute-start(f32[3,16,16,1]{3,1,0,2:T(8,128)} %get-tuple-element.142), channel_id=1, source_target_pairs={{0,8},{8,16},{16,24},{24,32},{32,40},{40,48},{48,56},{56,64},{64,7... | collective-permute-start | bytes 9224 | tf_op jit(solution)/shard_map/ppermute | solution.py:16
  316.9 64.8 %collective-permute-start.17 = (f32[3,16,16,1]{3,1,0,2:T(8,128)}, f32[3,16,16,1]{3,1,0,2:T(8,128)}, u32[]{:S(2)}, u32[]{:S(2)}) collective-permute-start(f32[3,16,16,1]{3,1,0,2:T(8,128)} %get-tuple-element.141), channel_id=1, source_target_pairs={{8,0},{16,8},{24,16},{32,24},{40,32},{48,40},{56,48},{64,56},{72,6... | collective-permute-start | bytes 9224 | tf_op jit(solution)/shard_map/ppermute | solution.py:19
  388.3 73.8 %copy-start.8 = (f32[16,16,128]{2,1,0:T(8,128)S(1)}, f32[16,16,128]{2,1,0:T(8,128)}, u32[]{:S(2)}) copy-start(f32[16,16,128]{2,1,0:T(8,128)} %copy.663) | copy-start | bytes 393220
  388.3 72.8 %collective-permute-start.22 = (f32[3,16,1,128]{3,1,0,2:T(8,128)S(1)}, f32[3,16,1,128]{3,1,0,2:T(8,128)S(1)}, u32[]{:S(2)}, u32[]{:S(2)}) collective-permute-start(f32[3,16,1,128]{3,1,0,2:T(8,128)S(1)} %get-tuple-element.138), channel_id=1, source_target_pairs={{0,1},{1,2},{2,3},{3,4},{4,5},{5,6},{6,7},{8,9},{9,10},{10,11},{11... | collective-permute-start | bytes 73736 | tf_op jit(solution)/shard_map/ppermute | solution.py:16
  394.4 66.7 %collective-permute-start.23 = (f32[3,16,1,128]{3,2,1,0:T(1,128)S(1)}, f32[3,16,1,128]{3,2,1,0:T(1,128)}, u32[]{:S(2)}, u32[]{:S(2)}) collective-permute-start(f32[3,16,1,128]{3,2,1,0:T(1,128)S(1)} %slice.756), channel_id=1, source_target_pairs={{1,0},{2,1},{3,2},{4,3},{5,4},{6,5},{7,6},{9,8},{10,9},{11,10},{12... | collective-permute-start | bytes 73736 | tf_op jit(solution)/shard_map/ppermute | solution.py:19
  395.7 63.8 %collective-permute-start.20 = (f32[3,16,16,1]{3,1,0,2:T(8,128)}, f32[3,16,16,1]{3,1,0,2:T(8,128)}, u32[]{:S(2)}, u32[]{:S(2)}) collective-permute-start(f32[3,16,16,1]{3,1,0,2:T(8,128)} %get-tuple-element.140), channel_id=1, source_target_pairs={{0,8},{8,16},{16,24},{24,32},{32,40},{40,48},{48,56},{56,64},{64,7... | collective-permute-start | bytes 9224 | tf_op jit(solution)/shard_map/ppermute | solution.py:16
  396.0 63.5 %collective-permute-start.21 = (f32[3,16,16,1]{3,1,0,2:T(8,128)S(1)}, f32[3,16,16,1]{3,1,0,2:T(8,128)}, u32[]{:S(2)}, u32[]{:S(2)}) collective-permute-start(f32[3,16,16,1]{3,1,0,2:T(8,128)S(1)} %get-tuple-element.139), channel_id=1, source_target_pairs={{8,0},{16,8},{24,16},{32,24},{40,32},{48,40},{56,48},{64,56},{72,6... | collective-permute-start | bytes 9224 | tf_op jit(solution)/shard_map/ppermute | solution.py:19
  446.6 15.9 %copy-start.5 = (f32[3,16,16,128]{3,1,0,2:T(8,128)S(1)}, f32[3,16,16,128]{3,1,0,2:T(8,128)}, u32[]{:S(2)}) copy-start(f32[3,16,16,128]{3,1,0,2:T(8,128)} %get-tuple-element.97) | copy-start | bytes 1179652
  465.2 72.6 %collective-permute-start.26 = (f32[3,16,1,128]{3,1,0,2:T(8,128)S(1)}, f32[3,16,1,128]{3,1,0,2:T(8,128)S(1)}, u32[]{:S(2)}, u32[]{:S(2)}) collective-permute-start(f32[3,16,1,128]{3,1,0,2:T(8,128)S(1)} %get-tuple-element.131), channel_id=1, source_target_pairs={{0,1},{1,2},{2,3},{3,4},{4,5},{5,6},{6,7},{8,9},{9,10},{10,11},{11... | collective-permute-start | bytes 73736 | tf_op jit(solution)/shard_map/ppermute | solution.py:16
  471.5 66.2 %collective-permute-start.27 = (f32[3,16,1,128]{3,1,0,2:T(8,128)S(1)}, f32[3,16,1,128]{3,1,0,2:T(8,128)S(1)}, u32[]{:S(2)}, u32[]{:S(2)}) collective-permute-start(f32[3,16,1,128]{3,1,0,2:T(8,128)S(1)} %get-tuple-element.132), channel_id=1, source_target_pairs={{1,0},{2,1},{3,2},{4,3},{5,4},{6,5},{7,6},{9,8},{10,9},{11,10},{12... | collective-permute-start | bytes 73736 | tf_op jit(solution)/shard_map/ppermute | solution.py:19
  472.8 63.5 %collective-permute-start.24 = (f32[3,16,16,1]{3,1,0,2:T(8,128)S(1)}, f32[3,16,16,1]{3,1,0,2:T(8,128)}, u32[]{:S(2)}, u32[]{:S(2)}) collective-permute-start(f32[3,16,16,1]{3,1,0,2:T(8,128)S(1)} %get-tuple-element.134), channel_id=1, source_target_pairs={{0,8},{8,16},{16,24},{24,32},{32,40},{40,48},{48,56},{56,64},{64,7... | collective-permute-start | bytes 9224 | tf_op jit(solution)/shard_map/ppermute | solution.py:16
  472.9 63.4 %collective-permute-start.25 = (f32[3,16,16,1]{3,1,0,2:T(8,128)S(1)}, f32[3,16,16,1]{3,1,0,2:T(8,128)}, u32[]{:S(2)}, u32[]{:S(2)}) collective-permute-start(f32[3,16,16,1]{3,1,0,2:T(8,128)S(1)} %get-tuple-element.133), channel_id=1, source_target_pairs={{8,0},{16,8},{24,16},{32,24},{40,32},{48,40},{56,48},{64,56},{72,6... | collective-permute-start | bytes 9224 | tf_op jit(solution)/shard_map/ppermute | solution.py:19
  540.6 68.9 %copy-start.15 = (pred[128]{0:T(512)(128)(4,1)S(1)}, pred[128]{0:T(512)(128)(4,1)}, u32[]{:S(2)}) copy-start(pred[128]{0:T(512)(128)(4,1)} %copy-done.12) | copy-start | bytes 388
  540.7 68.9 %copy-start.11 = (f32[3,16]{1,0:T(4,128)S(1)}, f32[3,16]{1,0:T(4,128)}, u32[]{:S(2)}) copy-start(f32[3,16]{1,0:T(4,128)} %param.34) | copy-start | bytes 580
  541.6 67.5 %collective-permute-start.30 = (f32[3,16,1,128]{3,1,0,2:T(8,128)S(1)}, f32[3,16,1,128]{3,1,0,2:T(8,128)S(1)}, u32[]{:S(2)}, u32[]{:S(2)}) collective-permute-start(f32[3,16,1,128]{3,1,0,2:T(8,128)S(1)} %get-tuple-element.121), channel_id=1, source_target_pairs={{0,1},{1,2},{2,3},{3,4},{4,5},{5,6},{6,7},{8,9},{9,10},{10,11},{11... | collective-permute-start | bytes 73736 | tf_op jit(solution)/shard_map/ppermute | solution.py:16
  548.0 61.2 %collective-permute-start.31 = (f32[3,16,1,128]{3,1,0,2:T(8,128)S(1)}, f32[3,16,1,128]{3,1,0,2:T(8,128)S(1)}, u32[]{:S(2)}, u32[]{:S(2)}) collective-permute-start(f32[3,16,1,128]{3,1,0,2:T(8,128)S(1)} %get-tuple-element.122), channel_id=1, source_target_pairs={{1,0},{2,1},{3,2},{4,3},{5,4},{6,5},{7,6},{9,8},{10,9},{11,10},{12... | collective-permute-start | bytes 73736 | tf_op jit(solution)/shard_map/ppermute | solution.py:19
  549.3 58.4 %collective-permute-start.28 = (f32[3,16,16,1]{3,1,0,2:T(8,128)}, f32[3,16,16,1]{3,1,0,2:T(8,128)}, u32[]{:S(2)}, u32[]{:S(2)}) collective-permute-start(f32[3,16,16,1]{3,1,0,2:T(8,128)} %get-tuple-element.124), channel_id=1, source_target_pairs={{0,8},{8,16},{16,24},{24,32},{32,40},{40,48},{48,56},{56,64},{64,7... | collective-permute-start | bytes 9224 | tf_op jit(solution)/shard_map/ppermute | solution.py:16
  549.4 58.4 %collective-permute-start.29 = (f32[3,16,16,1]{3,1,0,2:T(8,128)}, f32[3,16,16,1]{3,1,0,2:T(8,128)}, u32[]{:S(2)}, u32[]{:S(2)}) collective-permute-start(f32[3,16,16,1]{3,1,0,2:T(8,128)} %get-tuple-element.123), channel_id=1, source_target_pairs={{8,0},{16,8},{24,16},{32,24},{40,32},{48,40},{56,48},{64,56},{72,6... | collective-permute-start | bytes 9224 | tf_op jit(solution)/shard_map/ppermute | solution.py:19
  (1 other events, 14.4 us)
where the time goes:
time: 701 us; the launch traced here: 698 us
  blocking collectives  469 us (67%)
  local copies, waits for them, and re-layouts  115 us (16%)
  starting transfers between devices  63.9 us (9%)
  other arithmetic  42.6 us (6%)
    all_gather x7, blocking collectives, neighbours(): whole_top = lax.all_gather(top_row, 'lon', axis=2, tiled=True)  346 us
    psum x1, blocking collectives, on_device(): squares = lax.psum(jnp.sum(source_grad * source_grad), ('lon', 'lat'))  83.9 us
    ppermute x16, starting transfers between devices, with_halo(): lax.ppermute(lax.slice_in_dim(block, block.shape[dim] - width, None, axis...  47.4 us
    all_gather x7, local copies, waits for them, and re-layouts, neighbours(): whole_top = lax.all_gather(top_row, 'lon', axis=2, tiled=True)  46.9 us
    all_gather x1, blocking collectives, on_device(): fold_all = lax.all_gather(top_static, 'lon', axis=2, tiled=True)  39.1 us
    gather x14, local copies, waits for them, and re-layouts, neighbours(): partner_row = jnp.take(whole_top, fold_partner, axis=2)  37.4 us
    ppermute x16, starting transfers between devices, with_halo(): lax.ppermute(lax.slice_in_dim(block, 0, width, axis=dim), axis, backward)  16.5 us
  transfers between devices with their start and end apart: 32, of which 2 were waited for; matrix products, arithmetic and copies ran while one was open for 18% of the time, Pallas kernels for 0%

commit v1 on v0

--- a/solution.py
+++ b/solution.py
@@ -1,9 +1,21 @@
+import functools
 import jax
 import jax.numpy as jnp
 from jax import lax
 from jax.sharding import PartitionSpec as P
 
 STEPS = 4
+
+
+def render_the_joints(a0, k_dim):
+    oldest = lax.psum(1, axis_name="lon")
+    built = jnp.stack(oldest * [a0], axis=0)
+    opened = lax.all_to_all(built, axis_name="lon", split_axis=0, concat_axis=0)
+    odd = jnp.concatenate(opened, axis=k_dim)
+    return odd
+
+
+follow_results = functools.partial(render_the_joints, k_dim=2)
 
 
 def with_halo(block, sides, width, periodic):
@@ -57,7 +69,7 @@
         vertical_vel[:-1], 0.5 * (diffusivity[:-1] + diffusivity[1:]), ocean[:-1] * ocean[1:]
     )
     top_static = jnp.stack([north_vel[:, -1, :], diffusivity[:, -1, :], ocean[:, -1, :]])
-    fold_all = lax.all_gather(top_static, "lon", axis=2, tiled=True)
+    fold_all = follow_results(top_static)
     across = jnp.take(fold_all, fold_partner, axis=2)
     north_top = (lax.axis_index("lat") == lax.axis_size("lat") - 1).astype(jnp.float32)
     fold_own, fold_next = upwind_pair(

time: 701 us -> 675 us (0.963)
  blocking collectives: 469 us -> 437 us
  starting transfers between devices: 63.9 us -> 73.3 us
    all_gather x1 -> x0, blocking collectives: 39.1 us -> none  [on_device(): fold_all = lax.all_gather(top_static, 'lon', axis=2, tiled=True)]
    all_to_all x0 -> x1, starting transfers between devices: none -> 12.1 us  [render_the_joints(): opened = lax.all_to_all(built, axis_name='lon', split_axis=0, concat_axis=0)]
  transfers between devices with their start and end apart: 32 -> 33, of which waited for: 2 -> 1; matrix products, arithmetic and copies ran while one was open for 18% -> 17% of each run, Pallas kernels for 0% -> 0%
where the time goes in v1:
time: 675 us; the launch traced here: 672 us
  blocking collectives  437 us (65%)
  local copies, waits for them, and re-layouts  114 us (17%)
  starting transfers between devices  73.3 us (11%)
  other arithmetic  40.6 us (6%)
    all_gather x7, blocking collectives, neighbours(): whole_top = lax.all_gather(top_row, 'lon', axis=2, tiled=True)  351 us
    psum x1, blocking collectives, on_device(): squares = lax.psum(jnp.sum(source_grad * source_grad), ('lon', 'lat'))  85.9 us
    ppermute x16, starting transfers between devices, with_halo(): lax.ppermute(lax.slice_in_dim(block, block.shape[dim] - width, None, axis...  45.7 us
    all_gather x7, local copies, waits for them, and re-layouts, neighbours(): whole_top = lax.all_gather(top_row, 'lon', axis=2, tiled=True)  45.6 us
    gather x14, local copies, waits for them, and re-layouts, neighbours(): partner_row = jnp.take(whole_top, fold_partner, axis=2)  37.1 us
    ppermute x16, starting transfers between devices, with_halo(): lax.ppermute(lax.slice_in_dim(block, 0, width, axis=dim), axis, backward)  15.5 us
  transfers between devices with their start and end apart: 33, of which 1 were waited for; matrix products, arithmetic and copies ran while one was open for 17% of the time, Pallas kernels for 0%

profile of v1, /device:TPU:1, one launch (start us, length us, event | category | flops | bytes accessed | tf_op | source)
XLA Modules:
  0.0 671.6 jit_solution(8440913600586480073)
XLA Ops:
  0.7 2.0 fusion.105
  3.3 4.6 collective-permute-start.6
  15.9 12.1 %all-to-all-start = ((f32[32,3,16,128]{3,2,1,0:T(8,128)}), f32[32,3,16,128]{3,2,1,0:T(8,128)}, u32[]{:S(2)}, u32[]{:S(2)}) async-start(f32[32,3,16,128]{3,2,1,0:T(8,128)} %stack.17), calls=%async_computation | async-start | bytes 1572864 | tf_op jit(solution)/shard_map/all_to_all | solution.py:13
  29.4 1.4 collective-permute-start
  30.9 2.1 fusion.104
  33.0 55.3 %all-gather = f32[3,16,1,4096]{3,1,2,0:T(8,128)S(1)} all-gather(f32[3,16,1,128]{3,1,2,0:T(8,128)S(1)} %get-tuple-element.158), channel_id=2, replica_groups=mesh['lon'=32,'lat'=8] {'lon'}, dimensions={3}, use_global_device_ids=true | all-gather | bytes 811008 | tf_op jit(solution)/shard_map/all_gather | solution.py:86
  90.0 5.8 copy.558
  95.8 4.1 gather_fusion.1
  101.2 1.4 add_bitcast_fusion
  102.8 3.0 collective-permute-done.2
  105.8 4.9 collective-permute-start.4
  116.1 6.8 %copy.657 = f32[3,16,32,128]{1,0,3,2:T(4,128)} copy(f32[3,16,32,128]{3,1,0,2:T(8,128)} %bitcast.13) | data formatting | bytes 1572864 | tf_op jit(solution)/shard_map/reshape | solution.py:14
  122.9 4.1 gather_fusion
  128.1 2.8 multiply_add_fusion.2
  132.0 3.6 collective-permute-start.10
  137.0 47.8 %all-gather.1 = f32[3,16,1,4096]{3,1,2,0:T(8,128)} all-gather(f32[3,16,1,128]{3,1,2,0:T(8,128)S(1)} %get-tuple-element.153), channel_id=3, replica_groups=mesh['lon'=32,'lat'=8] {'lon'}, dimensions={3}, use_global_device_ids=true | all-gather | bytes 811008 | tf_op jit(solution)/shard_map/all_gather | solution.py:86
  184.7 1.7 collective-permute-start.8
  187.3 6.8 %copy.573 = f32[3,16,1,4096]{1,0,3,2:T(4,128)} copy(f32[3,16,1,4096]{3,1,2,0:T(8,128)} %all-gather.1) | data formatting | bytes 1572864 | tf_op jit(solution)/shard_map/all_gather | solution.py:86
  194.2 4.1 gather_fusion.2
  200.1 2.9 fusion.11
  204.9 4.3 collective-permute-start.14
  210.5 2.1 collective-permute-start.12
  212.6 2.1 collective-permute-start.13
  214.7 50.3 %all-gather.2 = f32[3,16,1,4096]{3,1,2,0:T(8,128)} all-gather(f32[3,16,1,128]{3,1,2,0:T(8,128)S(1)} %get-tuple-element.148), channel_id=4, replica_groups=mesh['lon'=32,'lat'=8] {'lon'}, dimensions={3}, use_global_device_ids=true | all-gather | bytes 811008 | tf_op jit(solution)/shard_map/all_gather | solution.py:86
  265.0 6.8 %copy.591 = f32[3,16,1,4096]{1,0,3,2:T(4,128)} copy(f32[3,16,1,4096]{3,1,2,0:T(8,128)} %all-gather.2) | data formatting | bytes 1572864 | tf_op jit(solution)/shard_map/all_gather | solution.py:86
  271.8 4.8 gather_fusion.3
  280.5 2.6 fusion.17
  285.1 4.9 collective-permute-start.18
  291.8 50.3 %all-gather.3 = f32[3,16,1,4096]{3,1,2,0:T(8,128)} all-gather(f32[3,16,1,128]{3,1,2,0:T(8,128)S(1)} %get-tuple-element.143), channel_id=5, replica_groups=mesh['lon'=32,'lat'=8] {'lon'}, dimensions={3}, use_global_device_ids=true | all-gather | bytes 811008 | tf_op jit(solution)/shard_map/all_gather | solution.py:86
  342.1 6.8 %copy.603 = f32[3,16,1,4096]{1,0,3,2:T(4,128)} copy(f32[3,16,1,4096]{3,1,2,0:T(8,128)} %all-gather.3) | data formatting | bytes 1572864 | tf_op jit(solution)/shard_map/all_gather | solution.py:86
  349.0 4.8 gather_fusion.4
  358.4 1.7 fusion.16
  361.6 5.1 collective-permute-start.22
  368.8 49.9 %all-gather.4 = f32[3,16,1,4096]{3,1,2,0:T(8,128)} all-gather(f32[3,16,1,128]{3,1,2,0:T(8,128)S(1)} %get-tuple-element.137), channel_id=6, replica_groups=mesh['lon'=32,'lat'=8] {'lon'}, dimensions={3}, use_global_device_ids=true | all-gather | bytes 811008 | tf_op jit(solution)/shard_map/all_gather | solution.py:86
  418.7 6.8 %copy.624 = f32[3,16,1,4096]{1,0,3,2:T(4,128)} copy(f32[3,16,1,4096]{3,1,2,0:T(8,128)} %all-gather.4) | data formatting | bytes 1572864 | tf_op jit(solution)/shard_map/all_gather | solution.py:86
  425.4 4.9 gather_fusion.5
  433.8 1.5 fusion.58
  436.6 6.4 collective-permute-start.26
  444.9 50.1 %all-gather.5 = f32[3,16,1,4096]{3,1,2,0:T(8,128)} all-gather(f32[3,16,1,128]{3,1,2,0:T(8,128)S(1)} %get-tuple-element.130), channel_id=7, replica_groups=mesh['lon'=32,'lat'=8] {'lon'}, dimensions={3}, use_global_device_ids=true | all-gather | bytes 811008 | tf_op jit(solution)/shard_map/all_gather | solution.py:86
  494.9 6.8 %copy.637 = f32[3,16,1,4096]{1,0,3,2:T(4,128)} copy(f32[3,16,1,4096]{3,1,2,0:T(8,128)} %all-gather.5) | data formatting | bytes 1572864 | tf_op jit(solution)/shard_map/all_gather | solution.py:86
  501.7 4.9 gather_fusion.6
  509.4 1.5 fusion.55
  513.0 6.4 collective-permute-start.30
  521.3 47.6 %all-gather.6 = f32[3,16,1,4096]{3,1,2,0:T(8,128)S(1)} all-gather(f32[3,16,1,128]{3,1,2,0:T(8,128)S(1)} %get-tuple-element.120), channel_id=8, replica_groups=mesh['lon'=32,'lat'=8] {'lon'}, dimensions={3}, use_global_device_ids=true | all-gather | bytes 811008 | tf_op jit(solution)/shard_map/all_gather | solution.py:86
  568.9 5.8 copy.651
  574.7 4.3 gather_fusion.7
  580.8 3.0 multiply_reduce_fusion
  583.9 85.9 %psum.7 = f32[]{:T(128)} all-reduce(f32[]{:T(128)} %get-tuple-element.93), channel_id=1, replica_groups=mesh['lon'=32,'lat'=8] {'lon','lat'}, use_global_device_ids=true, to_apply=%region_1.3 | all-reduce | flops 1 | bytes 8 | tf_op jit(solution)/shard_map/psum | solution.py:152
  (221 shorter events, 58.3 us)
Async XLA Ops:
  0.6 87.7 %copy-start = (f32[3,16,16,128]{3,2,1,0:T(8,128)S(1)}, f32[3,16,16,128]{3,2,1,0:T(8,128)}, u32[]{:S(2)}) copy-start(f32[3,16,16,128]{3,2,1,0:T(8,128)} %param.26) | copy-start | bytes 1179652
  0.7 87.7 %copy-start.32 = (s32[128]{0:T(128)S(1)}, s32[128]{0:T(128)}, u32[]{:S(2)}) copy-start(s32[128]{0:T(128)} %param.35) | copy-start | bytes 1540
  3.3 111.6 %collective-permute-start.6 = (f32[3,16,1,128]{3,1,0,2:T(8,128)}, f32[3,16,1,128]{3,1,0,2:T(8,128)}, u32[]{:S(2)}, u32[]{:S(2)}) collective-permute-start(f32[3,16,1,128]{3,1,0,2:T(8,128)} %get-tuple-element.160), channel_id=1, source_target_pairs={{0,1},{1,2},{2,3},{3,4},{4,5},{5,6},{6,7},{8,9},{9,10},{10,11},{11... | collective-permute-start | bytes 73736 | tf_op jit(solution)/shard_map/ppermute | solution.py:28
  7.9 106.9 %collective-permute-start.7 = (f32[3,16,1,128]{3,1,0,2:T(8,128)}, f32[3,16,1,128]{3,1,0,2:T(8,128)}, u32[]{:S(2)}, u32[]{:S(2)}) collective-permute-start(f32[3,16,1,128]{3,1,0,2:T(8,128)} %get-tuple-element.159), channel_id=1, source_target_pairs={{1,0},{2,1},{3,2},{4,3},{5,4},{6,5},{7,6},{9,8},{10,9},{11,10},{12... | collective-permute-start | bytes 73736 | tf_op jit(solution)/shard_map/ppermute | solution.py:31
  11.9 101.4 %collective-permute-start.5 = (f32[4,16,1,128]{3,2,1,0:T(1,128)}, f32[4,16,1,128]{3,2,1,0:T(1,128)}, u32[]{:S(2)}, u32[]{:S(2)}) collective-permute-start(f32[4,16,1,128]{3,2,1,0:T(1,128)} %get-tuple-element.119), channel_id=1, source_target_pairs={{1,0},{2,1},{3,2},{4,3},{5,4},{6,5},{7,6},{9,8},{10,9},{11,10},{12... | collective-permute-start | bytes 98312 | tf_op jit(solution)/shard_map/ppermute | solution.py:31
  15.9 100.2 %all-to-all-start = ((f32[32,3,16,128]{3,2,1,0:T(8,128)}), f32[32,3,16,128]{3,2,1,0:T(8,128)}, u32[]{:S(2)}, u32[]{:S(2)}) async-start(f32[32,3,16,128]{3,2,1,0:T(8,128)} %stack.17), calls=%async_computation | async-start | bytes 1572864 | tf_op jit(solution)/shard_map/all_to_all | solution.py:13
  29.1 72.1 %copy-start.13 = (f32[16,16,128]{2,1,0:T(8,128)S(1)}, f32[16,16,128]{2,1,0:T(8,128)}, u32[]{:S(2)}) copy-start(f32[16,16,128]{2,1,0:T(8,128)} %param.30) | copy-start | bytes 393220
  29.1 72.1 %copy-start.16 = (f32[16,16,128]{2,1,0:T(8,128)S(1)}, f32[16,16,128]{2,1,0:T(8,128)}, u32[]{:S(2)}) copy-start(f32[16,16,128]{2,1,0:T(8,128)} %param.29) | copy-start | bytes 393220
  29.1 71.6 %collective-permute-start.1 = (f32[4,16,16,1]{3,2,1,0:T(8,128)}, f32[4,16,16,1]{3,2,1,0:T(8,128)}, u32[]{:S(2)}, u32[]{:S(2)}) collective-permute-start(f32[4,16,16,1]{3,2,1,0:T(8,128)} %get-tuple-element.117), channel_id=1, source_target_pairs={{8,0},{16,8},{24,16},{32,24},{40,32},{48,40},{56,48},{64,56},{72,6... | collective-permute-start | bytes 12296 | tf_op jit(solution)/shard_map/ppermute | solution.py:31
  29.4 71.3 %collective-permute-start = (f32[4,16,16,1]{3,2,1,0:T(8,128)}, f32[4,16,16,1]{3,2,1,0:T(8,128)}, u32[]{:S(2)}, u32[]{:S(2)}) collective-permute-start(f32[4,16,16,1]{3,2,1,0:T(8,128)} %get-tuple-element.116), channel_id=1, source_target_pairs={{0,8},{8,16},{16,24},{24,32},{32,40},{40,48},{48,56},{56,64},{64,7... | collective-permute-start | bytes 12296 | tf_op jit(solution)/shard_map/ppermute | solution.py:28
  89.9 96.6 %copy-start.6 = (f32[15,16,128]{2,0,1:T(8,128)}, f32[15,16,128]{2,0,1:T(8,128)S(1)}, u32[]{:S(2)}) copy-start(f32[15,16,128]{2,0,1:T(8,128)S(1)} %copy.670) | copy-start | bytes 368644
  90.0 96.5 %copy-start.8 = (f32[15,16,128]{2,0,1:T(8,128)}, f32[15,16,128]{2,0,1:T(8,128)S(1)}, u32[]{:S(2)}) copy-start(f32[15,16,128]{2,0,1:T(8,128)S(1)} %copy.669) | copy-start | bytes 368644
  100.7 5.0 collective-permute-start.2
  100.7 9.9 %collective-permute-start.3 = (f32[3,16,16,1]{3,2,1,0:T(8,128)}, f32[3,16,16,1]{3,2,1,0:T(8,128)S(1)}, u32[]{:S(2)}, u32[]{:S(2)}) collective-permute-start(f32[3,16,16,1]{3,2,1,0:T(8,128)} %get-tuple-element.156), channel_id=1, source_target_pairs={{8,0},{16,8},{24,16},{32,24},{40,32},{48,40},{56,48},{64,56},{72,6... | collective-permute-start | bytes 9224 | tf_op jit(solution)/shard_map/ppermute | solution.py:31
  105.8 7.6 %collective-permute-start.4 = (f32[4,16,1,128]{3,2,1,0:T(1,128)}, f32[4,16,1,128]{3,2,1,0:T(1,128)S(1)}, u32[]{:S(2)}, u32[]{:S(2)}) collective-permute-start(f32[4,16,1,128]{3,2,1,0:T(1,128)} %get-tuple-element.118), channel_id=1, source_target_pairs={{0,1},{1,2},{2,3},{3,4},{4,5},{5,6},{6,7},{8,9},{9,10},{10,11},{11... | collective-permute-start | bytes 98312 | tf_op jit(solution)/shard_map/ppermute | solution.py:28
  127.3 231.1 %copy-start.14 = (f32[16,128]{1,0:T(8,128)}, f32[16,128]{1,0:T(8,128)S(1)}, u32[]{:S(2)}) copy-start(f32[16,128]{1,0:T(8,128)S(1)} %get-tuple-element.101) | copy-start | bytes 24580
  132.0 68.0 %collective-permute-start.10 = (f32[3,16,1,128]{3,1,0,2:T(8,128)S(1)}, f32[3,16,1,128]{3,1,0,2:T(8,128)S(1)}, u32[]{:S(2)}, u32[]{:S(2)}) collective-permute-start(f32[3,16,1,128]{3,1,0,2:T(8,128)S(1)} %get-tuple-element.155), channel_id=1, source_target_pairs={{0,1},{1,2},{2,3},{3,4},{4,5},{5,6},{6,7},{8,9},{9,10},{10,11},{11... | collective-permute-start | bytes 73736 | tf_op jit(solution)/shard_map/ppermute | solution.py:28
  135.7 64.3 %collective-permute-start.11 = (f32[3,16,1,128]{3,1,0,2:T(8,128)S(1)}, f32[3,16,1,128]{3,1,0,2:T(8,128)S(1)}, u32[]{:S(2)}, u32[]{:S(2)}) collective-permute-start(f32[3,16,1,128]{3,1,0,2:T(8,128)S(1)} %get-tuple-element.154), channel_id=1, source_target_pairs={{1,0},{2,1},{3,2},{4,3},{5,4},{6,5},{7,6},{9,8},{10,9},{11,10},{12... | collective-permute-start | bytes 73736 | tf_op jit(solution)/shard_map/ppermute | solution.py:31
  137.0 63.1 %copy-start.26 = (f32[3,16]{1,0:T(4,128)S(1)}, f32[3,16]{1,0:T(4,128)}, u32[]{:S(2)}) copy-start(f32[3,16]{1,0:T(4,128)} %param.34) | copy-start | bytes 580
  184.7 13.7 %collective-permute-start.8 = (f32[3,16,16,1]{3,2,1,0:T(8,128)}, f32[3,16,16,1]{3,2,1,0:T(8,128)}, u32[]{:S(2)}, u32[]{:S(2)}) collective-permute-start(f32[3,16,16,1]{3,2,1,0:T(8,128)} %get-tuple-element.152), channel_id=1, source_target_pairs={{0,8},{8,16},{16,24},{24,32},{32,40},{40,48},{48,56},{56,64},{64,7... | collective-permute-start | bytes 9224 | tf_op jit(solution)/shard_map/ppermute | solution.py:28
  186.5 11.9 %collective-permute-start.9 = (f32[3,16,16,1]{3,2,1,0:T(8,128)}, f32[3,16,16,1]{3,2,1,0:T(8,128)}, u32[]{:S(2)}, u32[]{:S(2)}) collective-permute-start(f32[3,16,16,1]{3,2,1,0:T(8,128)} %get-tuple-element.151), channel_id=1, source_target_pairs={{8,0},{16,8},{24,16},{32,24},{40,32},{48,40},{56,48},{64,56},{72,6... | collective-permute-start | bytes 9224 | tf_op jit(solution)/shard_map/ppermute | solution.py:31
  204.9 75.5 %collective-permute-start.14 = (f32[3,16,1,128]{3,1,0,2:T(8,128)S(1)}, f32[3,16,1,128]{3,1,0,2:T(8,128)S(1)}, u32[]{:S(2)}, u32[]{:S(2)}) collective-permute-start(f32[3,16,1,128]{3,1,0,2:T(8,128)S(1)} %get-tuple-element.150), channel_id=1, source_target_pairs={{0,1},{1,2},{2,3},{3,4},{4,5},{5,6},{6,7},{8,9},{9,10},{10,11},{11... | collective-permute-start | bytes 73736 | tf_op jit(solution)/shard_map/ppermute | solution.py:28
  209.2 71.2 %collective-permute-start.15 = (f32[3,16,1,128]{3,1,0,2:T(8,128)S(1)}, f32[3,16,1,128]{3,1,0,2:T(8,128)S(1)}, u32[]{:S(2)}, u32[]{:S(2)}) collective-permute-start(f32[3,16,1,128]{3,1,0,2:T(8,128)S(1)} %get-tuple-element.149), channel_id=1, source_target_pairs={{1,0},{2,1},{3,2},{4,3},{5,4},{6,5},{7,6},{9,8},{10,9},{11,10},{12... | collective-permute-start | bytes 73736 | tf_op jit(solution)/shard_map/ppermute | solution.py:31
  210.5 67.2 %collective-permute-start.12 = (f32[3,16,16,1]{3,1,0,2:T(8,128)}, f32[3,16,16,1]{3,1,0,2:T(8,128)}, u32[]{:S(2)}, u32[]{:S(2)}) collective-permute-start(f32[3,16,16,1]{3,1,0,2:T(8,128)} %get-tuple-element.147), channel_id=1, source_target_pairs={{0,8},{8,16},{16,24},{24,32},{32,40},{40,48},{48,56},{56,64},{64,7... | collective-permute-start | bytes 9224 | tf_op jit(solution)/shard_map/ppermute | solution.py:28
  212.6 66.2 %collective-permute-start.13 = (f32[3,16,16,1]{3,1,0,2:T(8,128)}, f32[3,16,16,1]{3,1,0,2:T(8,128)}, u32[]{:S(2)}, u32[]{:S(2)}) collective-permute-start(f32[3,16,16,1]{3,1,0,2:T(8,128)} %get-tuple-element.146), channel_id=1, source_target_pairs={{8,0},{16,8},{24,16},{32,24},{40,32},{48,40},{56,48},{64,56},{72,6... | collective-permute-start | bytes 9224 | tf_op jit(solution)/shard_map/ppermute | solution.py:31
  285.1 72.5 %collective-permute-start.18 = (f32[3,16,1,128]{3,1,0,2:T(8,128)S(1)}, f32[3,16,1,128]{3,1,0,2:T(8,128)}, u32[]{:S(2)}, u32[]{:S(2)}) collective-permute-start(f32[3,16,1,128]{3,1,0,2:T(8,128)S(1)} %get-tuple-element.145), channel_id=1, source_target_pairs={{0,1},{1,2},{2,3},{3,4},{4,5},{5,6},{6,7},{8,9},{9,10},{10,11},{11... | collective-permute-start | bytes 73736 | tf_op jit(solution)/shard_map/ppermute | solution.py:28
  289.9 67.7 %collective-permute-start.19 = (f32[3,16,1,128]{3,1,0,2:T(8,128)S(1)}, f32[3,16,1,128]{3,1,0,2:T(8,128)}, u32[]{:S(2)}, u32[]{:S(2)}) collective-permute-start(f32[3,16,1,128]{3,1,0,2:T(8,128)S(1)} %get-tuple-element.144), channel_id=1, source_target_pairs={{1,0},{2,1},{3,2},{4,3},{5,4},{6,5},{7,6},{9,8},{10,9},{11,10},{12... | collective-permute-start | bytes 73736 | tf_op jit(solution)/shard_map/ppermute | solution.py:31
  291.2 63.6 %collective-permute-start.16 = (f32[3,16,16,1]{3,1,0,2:T(8,128)}, f32[3,16,16,1]{3,1,0,2:T(8,128)}, u32[]{:S(2)}, u32[]{:S(2)}) collective-permute-start(f32[3,16,16,1]{3,1,0,2:T(8,128)} %get-tuple-element.142), channel_id=1, source_target_pairs={{0,8},{8,16},{16,24},{24,32},{32,40},{40,48},{48,56},{56,64},{64,7... | collective-permute-start | bytes 9224 | tf_op jit(solution)/shard_map/ppermute | solution.py:28
  291.3 64.7 %collective-permute-start.17 = (f32[3,16,16,1]{3,1,0,2:T(8,128)}, f32[3,16,16,1]{3,1,0,2:T(8,128)}, u32[]{:S(2)}, u32[]{:S(2)}) collective-permute-start(f32[3,16,16,1]{3,1,0,2:T(8,128)} %get-tuple-element.141), channel_id=1, source_target_pairs={{8,0},{16,8},{24,16},{32,24},{40,32},{48,40},{56,48},{64,56},{72,6... | collective-permute-start | bytes 9224 | tf_op jit(solution)/shard_map/ppermute | solution.py:31
  360.1 71.3 %copy-start.15 = (f32[16,128]{1,0:T(8,128)S(1)}, f32[16,128]{1,0:T(8,128)}, u32[]{:S(2)}) copy-start(f32[16,128]{1,0:T(8,128)} %copy-done.14) | copy-start | bytes 24580
  360.1 71.3 %copy-start.29 = (pred[128]{0:T(512)(128)(4,1)S(1)}, pred[128]{0:T(512)(128)(4,1)}, u32[]{:S(2)}) copy-start(pred[128]{0:T(512)(128)(4,1)} %compare_and_fusion) | copy-start | bytes 388
  360.2 72.6 %copy-start.4 = (f32[16,16,128]{2,0,1:T(8,128)S(1)}, f32[16,16,128]{2,0,1:T(8,128)}, u32[]{:S(2)}) copy-start(f32[16,16,128]{2,0,1:T(8,128)} %copy.616) | copy-start | bytes 393220
  360.3 72.6 %copy-start.5 = (f32[16,16,128]{2,0,1:T(8,128)S(1)}, f32[16,16,128]{2,0,1:T(8,128)}, u32[]{:S(2)}) copy-start(f32[16,16,128]{2,0,1:T(8,128)} %copy.611) | copy-start | bytes 393220
  361.6 71.8 %copy-start.17 = (f32[16,16,128]{2,1,0:T(8,128)S(1)}, f32[16,16,128]{2,1,0:T(8,128)}, u32[]{:S(2)}) copy-start(f32[16,16,128]{2,1,0:T(8,128)} %copy.671) | copy-start | bytes 393220
  361.6 71.5 %collective-permute-start.22 = (f32[3,16,1,128]{3,1,0,2:T(8,128)S(1)}, f32[3,16,1,128]{3,1,0,2:T(8,128)S(1)}, u32[]{:S(2)}, u32[]{:S(2)}) collective-permute-start(f32[3,16,1,128]{3,1,0,2:T(8,128)S(1)} %get-tuple-element.138), channel_id=1, source_target_pairs={{0,1},{1,2},{2,3},{3,4},{4,5},{5,6},{6,7},{8,9},{9,10},{10,11},{11... | collective-permute-start | bytes 73736 | tf_op jit(solution)/shard_map/ppermute | solution.py:28
  366.7 66.4 %collective-permute-start.23 = (f32[3,16,1,128]{3,2,1,0:T(1,128)S(1)}, f32[3,16,1,128]{3,2,1,0:T(1,128)S(1)}, u32[]{:S(2)}, u32[]{:S(2)}) collective-permute-start(f32[3,16,1,128]{3,2,1,0:T(1,128)S(1)} %slice.756), channel_id=1, source_target_pairs={{1,0},{2,1},{3,2},{4,3},{5,4},{6,5},{7,6},{9,8},{10,9},{11,10},{12... | collective-permute-start | bytes 73736 | tf_op jit(solution)/shard_map/ppermute | solution.py:31
  368.0 63.5 %collective-permute-start.20 = (f32[3,16,16,1]{3,1,0,2:T(8,128)S(1)}, f32[3,16,16,1]{3,1,0,2:T(8,128)}, u32[]{:S(2)}, u32[]{:S(2)}) collective-permute-start(f32[3,16,16,1]{3,1,0,2:T(8,128)S(1)} %get-tuple-element.140), channel_id=1, source_target_pairs={{0,8},{8,16},{16,24},{24,32},{32,40},{40,48},{48,56},{56,64},{64,7... | collective-permute-start | bytes 9224 | tf_op jit(solution)/shard_map/ppermute | solution.py:28
  368.1 63.4 %collective-permute-start.21 = (f32[3,16,16,1]{3,1,0,2:T(8,128)S(1)}, f32[3,16,16,1]{3,1,0,2:T(8,128)}, u32[]{:S(2)}, u32[]{:S(2)}) collective-permute-start(f32[3,16,16,1]{3,1,0,2:T(8,128)S(1)} %get-tuple-element.139), channel_id=1, source_target_pairs={{8,0},{16,8},{24,16},{32,24},{40,32},{48,40},{56,48},{64,56},{72,6... | collective-permute-start | bytes 9224 | tf_op jit(solution)/shard_map/ppermute | solution.py:31
  435.4 73.8 %copy-start.3 = (f32[16,16,128]{2,0,1:T(8,128)S(1)}, f32[16,16,128]{2,0,1:T(8,128)}, u32[]{:S(2)}) copy-start(f32[16,16,128]{2,0,1:T(8,128)} %copy-done.2) | copy-start | bytes 393220
  436.6 72.6 %collective-permute-start.26 = (f32[3,16,1,128]{3,1,0,2:T(8,128)S(1)}, f32[3,16,1,128]{3,1,0,2:T(8,128)S(1)}, u32[]{:S(2)}, u32[]{:S(2)}) collective-permute-start(f32[3,16,1,128]{3,1,0,2:T(8,128)S(1)} %get-tuple-element.131), channel_id=1, source_target_pairs={{0,1},{1,2},{2,3},{3,4},{4,5},{5,6},{6,7},{8,9},{9,10},{10,11},{11... | collective-permute-start | bytes 73736 | tf_op jit(solution)/shard_map/ppermute | solution.py:28
  443.0 66.2 %collective-permute-start.27 = (f32[3,16,1,128]{3,1,0,2:T(8,128)S(1)}, f32[3,16,1,128]{3,1,0,2:T(8,128)S(1)}, u32[]{:S(2)}, u32[]{:S(2)}) collective-permute-start(f32[3,16,1,128]{3,1,0,2:T(8,128)S(1)} %get-tuple-element.132), channel_id=1, source_target_pairs={{1,0},{2,1},{3,2},{4,3},{5,4},{6,5},{7,6},{9,8},{10,9},{11,10},{12... | collective-permute-start | bytes 73736 | tf_op jit(solution)/shard_map/ppermute | solution.py:31
  444.3 63.5 %collective-permute-start.24 = (f32[3,16,16,1]{3,1,0,2:T(8,128)S(1)}, f32[3,16,16,1]{3,1,0,2:T(8,128)}, u32[]{:S(2)}, u32[]{:S(2)}) collective-permute-start(f32[3,16,16,1]{3,1,0,2:T(8,128)S(1)} %get-tuple-element.134), channel_id=1, source_target_pairs={{0,8},{8,16},{16,24},{24,32},{32,40},{40,48},{48,56},{56,64},{64,7... | collective-permute-start | bytes 9224 | tf_op jit(solution)/shard_map/ppermute | solution.py:28
  444.3 63.4 %collective-permute-start.25 = (f32[3,16,16,1]{3,1,0,2:T(8,128)S(1)}, f32[3,16,16,1]{3,1,0,2:T(8,128)}, u32[]{:S(2)}, u32[]{:S(2)}) collective-permute-start(f32[3,16,16,1]{3,1,0,2:T(8,128)S(1)} %get-tuple-element.133), channel_id=1, source_target_pairs={{8,0},{16,8},{24,16},{32,24},{40,32},{48,40},{56,48},{64,56},{72,6... | collective-permute-start | bytes 9224 | tf_op jit(solution)/shard_map/ppermute | solution.py:31
  512.0 68.8 %copy-start.27 = (f32[3,16]{1,0:T(4,128)S(1)}, f32[3,16]{1,0:T(4,128)}, u32[]{:S(2)}) copy-start(f32[3,16]{1,0:T(4,128)} %param.34) | copy-start | bytes 580
  513.0 67.5 %collective-permute-start.30 = (f32[3,16,1,128]{3,1,0,2:T(8,128)S(1)}, f32[3,16,1,128]{3,1,0,2:T(8,128)S(1)}, u32[]{:S(2)}, u32[]{:S(2)}) collective-permute-start(f32[3,16,1,128]{3,1,0,2:T(8,128)S(1)} %get-tuple-element.121), channel_id=1, source_target_pairs={{0,1},{1,2},{2,3},{3,4},{4,5},{5,6},{6,7},{8,9},{9,10},{10,11},{11... | collective-permute-start | bytes 73736 | tf_op jit(solution)/shard_map/ppermute | solution.py:28
  519.4 61.1 %collective-permute-start.31 = (f32[3,16,1,128]{3,1,0,2:T(8,128)S(1)}, f32[3,16,1,128]{3,1,0,2:T(8,128)S(1)}, u32[]{:S(2)}, u32[]{:S(2)}) collective-permute-start(f32[3,16,1,128]{3,1,0,2:T(8,128)S(1)} %get-tuple-element.122), channel_id=1, source_target_pairs={{1,0},{2,1},{3,2},{4,3},{5,4},{6,5},{7,6},{9,8},{10,9},{11,10},{12... | collective-permute-start | bytes 73736 | tf_op jit(solution)/shard_map/ppermute | solution.py:31
  520.7 58.4 %collective-permute-start.28 = (f32[3,16,16,1]{3,1,0,2:T(8,128)}, f32[3,16,16,1]{3,1,0,2:T(8,128)}, u32[]{:S(2)}, u32[]{:S(2)}) collective-permute-start(f32[3,16,16,1]{3,1,0,2:T(8,128)} %get-tuple-element.124), channel_id=1, source_target_pairs={{0,8},{8,16},{16,24},{24,32},{32,40},{40,48},{48,56},{56,64},{64,7... | collective-permute-start | bytes 9224 | tf_op jit(solution)/shard_map/ppermute | solution.py:28
  520.8 58.3 %collective-permute-start.29 = (f32[3,16,16,1]{3,1,0,2:T(8,128)}, f32[3,16,16,1]{3,1,0,2:T(8,128)}, u32[]{:S(2)}, u32[]{:S(2)}) collective-permute-start(f32[3,16,16,1]{3,1,0,2:T(8,128)} %get-tuple-element.123), channel_id=1, source_target_pairs={{8,0},{16,8},{24,16},{32,24},{40,32},{48,40},{56,48},{64,56},{72,6... | collective-permute-start | bytes 9224 | tf_op jit(solution)/shard_map/ppermute | solution.py:31
  (18 other events, 347.0 us)
